TPU v7x, 256 devices: a whole 4x4x8 slice. The times are simulated.
256 devices in a mesh: embed: 8 (over x, core), hidden: 32 (over y, z).
Axes of the slice: x: 4, y: 4, z: 8, core: 2. Of those that a mesh axis runs over, the one named last changes fastest.
Arguments:
- rows_in: bfloat16 [512, 16384], P('hidden', 'embed'), may hold values from -6 to 6
- gate_weight: bfloat16 [16384, 28672], P('embed', 'hidden'), may hold values from -0.046875 to 0.046875
- up_weight: bfloat16 [16384, 28672], P('embed', 'hidden'), may hold values from -0.046875 to 0.046875
- down_weight: bfloat16 [28672, 16384], P('hidden', 'embed'), may hold values from -0.03125 to 0.03125
Outputs:
- rows_out: bfloat16 [512, 16384], P('hidden', 'embed')
All inputs are finite; a program needn't handle non-finite values.
Results may differ from a plain program's by a relative error of at most 0.0049.
Values may be sent and summed in bfloat16 or wider, within the bound.
No kernel may reach another device: no remote copies, remote signals or barrier semaphores. Data moves between devices by JAX's collectives and lax.ppermute only.
A program may use at most 64 MiB of HBM per device.

v0:
```python
import jax
import jax.numpy as jnp
from jax import lax
from jax.sharding import Mesh, PartitionSpec as P


def on_device(rows_in, gate_weight, up_weight, down_weight):
    width = gate_weight.shape[1]
    piece = lax.all_gather(rows_in, "hz", axis=0, tiled=True)
    piece = lax.all_gather(piece, "hy", axis=0, tiled=True)
    gate_part = jnp.dot(piece, gate_weight, preferred_element_type=jnp.float32)
    up_part = jnp.dot(piece, up_weight, preferred_element_type=jnp.float32)
    partial_value = jnp.concatenate([gate_part, up_part], axis=1)
    summed = lax.psum_scatter(partial_value, "embed", scatter_dimension=0, tiled=True)
    activated = (jax.nn.silu(summed[:, :width]) * summed[:, width:]).astype(jnp.bfloat16)
    activated = lax.all_gather(activated, "embed", axis=0, tiled=True)
    partial_out = jnp.dot(activated, down_weight, preferred_element_type=jnp.float32)
    totals = lax.psum_scatter(partial_out, "hy", scatter_dimension=0, tiled=True)
    totals = lax.psum_scatter(totals, "hz", scatter_dimension=0, tiled=True)
    return totals.astype(jnp.bfloat16)


def solution(mesh):
    embed, hidden = (mesh.shape["embed"], mesh.shape["hidden"])
    ny = {d.coords[1] for d in mesh.devices.flat}
    ny = len(ny)
    sub = Mesh(mesh.devices.reshape(embed, ny, hidden // ny), ("embed", "hy", "hz"))
    rows = P(("hy", "hz"), "embed")
    weights = P("embed", ("hy", "hz"))
    placed = (rows, weights, weights, P(("hy", "hz"), "embed"))
    return jax.shard_map(on_device, mesh=sub, in_specs=placed, out_specs=rows, check_vma=False)
```

profile of v0, /device:TPU:2, one launch (start us, length us, event | category | flops | bytes accessed | tf_op | source)
XLA Modules:
  0.0 239.4 jit_solution(16744164856222922656)
XLA Ops:
  6.5 0.0 all-gather.2.cloned.1.call-start
  6.5 31.1 %all_gather.9 = bf16[128,2048]{1,0:T(8,128)(2,1)} all-gather(bf16[16,2048]{1,0:T(8,128)(2,1)} %param.4), channel_id=1, replica_groups=mesh['embed'=8,'hy'=4,'hz'=8] {'hz'}, dimensions={0}, use_global_device_ids=true | all-gather | bytes 589824 | tf_op jit(solution)/shard_map/all_gather | solution.py:9
  37.6 0.0 all-gather.2.cloned.1.call-update
  37.7 0.0 reduce-scatter.4.cloned.1.call-start
  37.7 33.1 %all-gather.2.cloned.1.call-done = bf16[512,2048]{1,0:T(8,128)(2,1)} async-done(((bf16[128,2048]{1,0:T(8,128)(2,1)}), bf16[512,2048]{1,0:T(8,128)(2,1)}) %all-gather.2.cloned.1.call-update) | async-done | bytes 2097168 | tf_op jit(solution)/shard_map/all_gather | solution.py:10
  70.8 0.0 copy-start
  70.8 0.0 copy-start.1
  70.8 5.1 %fusion.2 = f32[512,896]{1,0:T(8,128)S(1)} fusion(bf16[512,2048]{1,0:T(8,128)(2,1)} %all-gather.2.cloned.1.call-done, bf16[2048,896]{1,0:T(8,128)(2,1)} %param.6), kind=kOutput, calls=%fused_computation.4 | convolution fusion | flops 1879048192 | bytes 7602176 | tf_op jit(solution)/shard_map/dot_general | solution.py:12
  75.9 0.0 copy-done
  75.9 0.0 copy-done.1
  76.0 2.3 fusion.1
  78.3 2.1 pad_maximum_fusion
  80.3 0.0 reduce-scatter.4.cloned.1.call-update
  80.4 0.0 reduce-scatter.6.cloned.1.call-start
  80.4 36.1 %reduce-scatter.4.cloned.1.call-done = f32[64,1792]{1,0:T(8,128)} async-done(((f32[512,1792]{1,0:T(8,128)}), f32[64,1792]{1,0:T(8,128)}) %reduce-scatter.4.cloned.1.call-update) | async-done | bytes 458768 | tf_op jit(solution)/shard_map/reduce_scatter | solution.py:14
  116.5 1.1 fusion
  117.6 15.1 %all_gather.11 = bf16[512,896]{1,0:T(8,128)(2,1)S(1)} all-gather(bf16[64,896]{1,0:T(8,128)(2,1)S(1)} %fusion), channel_id=1, replica_groups=mesh['embed'=8,'hy'=4,'hz'=8] {'embed'}, dimensions={0}, use_global_device_ids=true | all-gather | bytes 1032192 | tf_op jit(solution)/shard_map/all_gather | solution.py:16
  132.7 6.3 %fusion.3 = f32[512,2048]{1,0:T(8,128)} fusion(bf16[512,896]{1,0:T(8,128)(2,1)S(1)} %all_gather.11, bf16[896,2048]{1,0:T(8,128)(2,1)} %param.7), kind=kOutput, calls=%fused_computation.5 | convolution fusion | flops 1879048192 | bytes 8781824 | tf_op jit(solution)/shard_map/dot_general | solution.py:17
  139.0 0.0 reduce-scatter.6.cloned.1.call-update
  139.1 0.0 reduce-scatter.8.cloned.1.call-start
  139.1 51.3 %reduce-scatter.6.cloned.1.call-done = f32[128,2048]{1,0:T(8,128)} async-done(((f32[512,2048]{1,0:T(8,128)}), f32[128,2048]{1,0:T(8,128)}) %reduce-scatter.6.cloned.1.call-update) | async-done | bytes 1048592 | tf_op jit(solution)/shard_map/reduce_scatter | solution.py:18
  190.4 0.0 reduce-scatter.8.cloned.1.call-update
  190.4 40.9 %reduce-scatter.8.cloned.1.call-done = f32[16,2048]{1,0:T(8,128)} async-done(((f32[128,2048]{1,0:T(8,128)}), f32[16,2048]{1,0:T(8,128)}) %reduce-scatter.8.cloned.1.call-update) | async-done | bytes 131088 | tf_op jit(solution)/shard_map/reduce_scatter | solution.py:19
  231.4 1.5 convert_element_type.7
Async XLA Ops:
  6.5 64.2 %all-gather.2.cloned.1.call-start = ((), (), s32[]{:S(2)}) async-start(), calls=%async_computation.3 | async-start | bytes 2621440 | tf_op jit(solution)/shard_map/all_gather | solution.py:10
  37.7 78.9 %reduce-scatter.4.cloned.1.call-start = ((), (), s32[]{:S(2)}) async-start(), calls=%async_computation.4 | async-start | bytes 4128768 | tf_op jit(solution)/shard_map/reduce_scatter | solution.py:14
  70.8 5.2 %copy-start = (bf16[2048,896]{1,0:T(8,128)(2,1)S(1)}, bf16[2048,896]{1,0:T(8,128)(2,1)}, u32[]{:S(2)}) copy-start(bf16[2048,896]{1,0:T(8,128)(2,1)} %param.5) | copy-start | bytes 11010052
  70.8 5.2 %copy-start.1 = (bf16[512,2048]{1,0:T(8,128)(2,1)S(1)}, bf16[512,2048]{1,0:T(8,128)(2,1)}, u32[]{:S(2)}) copy-start(bf16[512,2048]{1,0:T(8,128)(2,1)} %all-gather.2.cloned.1.call-done) | copy-start | bytes 6291460
  80.4 110.0 %reduce-scatter.6.cloned.1.call-start = ((), (), s32[]{:S(2)}) async-start(), calls=%async_computation.5 | async-start | bytes 5242880 | tf_op jit(solution)/shard_map/reduce_scatter | solution.py:18
  139.1 92.3 %reduce-scatter.8.cloned.1.call-start = ((), (), s32[]{:S(2)}) async-start(), calls=%async_computation.6 | async-start | bytes 1179648 | tf_op jit(solution)/shard_map/reduce_scatter | solution.py:19
Sparse Core Ops, SparseCore 0:
  37.8 32.9 all-gather.1
  80.5 35.9 reduce-scatter.3
  139.2 51.1 reduce-scatter.5
  192.9 38.3 reduce-scatter.7
where the time goes:
time: 240 us; the launch traced here: 239 us
  waiting for transfers between devices  161 us (67%)
  blocking collectives  46.2 us (19%)
  matrix products  13.8 us (6%)
  between operations  13.2 us (6%)
  other arithmetic  4.72 us (2%)
    reduce_scatter x1, waiting for transfers between devices, on_device(): lax.psum_scatter(partial_out, 'hy', scatter_dimension=0, tiled=True)  51.3 us
    reduce_scatter x1, waiting for transfers between devices, on_device(): totals = lax.psum_scatter(totals, 'hz', scatter_dimension=0, tiled=True)  40.9 us
    reduce_scatter x1, waiting for transfers between devices, on_device(): lax.psum_scatter(partial_value, 'embed', scatter_dimension=0, tiled=True)  36.1 us
    all_gather x1, waiting for transfers between devices, on_device(): piece = lax.all_gather(piece, 'hy', axis=0, tiled=True)  33.1 us
    all_gather x1, blocking collectives, on_device(): piece = lax.all_gather(rows_in, 'hz', axis=0, tiled=True)  31.1 us
    all_gather x1, blocking collectives, on_device(): activated = lax.all_gather(activated, 'embed', axis=0, tiled=True)  15.1 us
    dot_general x1, matrix products, on_device(): jnp.dot(activated, down_weight, preferred_element_type=jnp.float32)  6.35 us
    dot_general x1, matrix products, on_device(): up_part = jnp.dot(piece, up_weight, preferred_element_type=jnp.float32)  5.14 us
  transfers between devices with their start and end apart: 4, of which 4 were waited for; matrix products, arithmetic and copies ran while one was open for 0% of the time, Pallas kernels for 0%

commit v1 on v0

--- a/solution.py
+++ b/solution.py
@@ -2,6 +2,12 @@
 import jax.numpy as jnp
 from jax import lax
 from jax.sharding import Mesh, PartitionSpec as P
+
+
+def joined_along(parts, dim):
+    shape = list(parts.shape[1:])
+    shape[dim] *= parts.shape[0]
+    return jnp.moveaxis(parts, 0, dim).reshape(shape)
 
 
 def on_device(rows_in, gate_weight, up_weight, down_weight):
@@ -13,7 +19,19 @@
     partial_value = jnp.concatenate([gate_part, up_part], axis=1)
     summed = lax.psum_scatter(partial_value, "embed", scatter_dimension=0, tiled=True)
     activated = (jax.nn.silu(summed[:, :width]) * summed[:, width:]).astype(jnp.bfloat16)
-    activated = lax.all_gather(activated, "embed", axis=0, tiled=True)
+    length = lax.axis_size("embed")
+    pairs = [(i, (i + 1) % length) for i in range(length)]
+    back = [(b, a) for a, b in pairs]
+    lower, upper = ([], [])
+    for lap in range(length - 1):
+        if lap % 2 == 0:
+            lower.append(lax.ppermute(lower[-1] if lower else activated, "embed", pairs))
+        else:
+            upper.append(lax.ppermute(upper[-1] if upper else activated, "embed", back))
+    blocks = jnp.stack([*lower[::-1], activated, *upper])
+    shift = lax.axis_index("embed") - len(lower)
+    blocks = blocks[(jnp.arange(length) - shift) % length]
+    activated = joined_along(blocks, 0)
     partial_out = jnp.dot(activated, down_weight, preferred_element_type=jnp.float32)
     totals = lax.psum_scatter(partial_out, "hy", scatter_dimension=0, tiled=True)
     totals = lax.psum_scatter(totals, "hz", scatter_dimension=0, tiled=True)

time: 240 us -> 250 us (1.042)
  waiting for transfers between devices: 161 us -> 178 us
  blocking collectives: 46.2 us -> 31.1 us
  starting transfers between devices: 0.13 us -> 7.03 us
    all_gather x1 -> x0, blocking collectives: 15.1 us -> none  [on_device(): activated = lax.all_gather(activated, 'embed', axis=0, tiled=True)]
    ppermute x0 -> x7, waiting for transfers between devices: none -> 11.3 us  [the longest x4 11.3 us: on_device(): lax.ppermute(lower[-1] if lower else activated, 'embed', pairs)]
    ppermute x0 -> x7, starting transfers between devices: none -> 6.91 us  [the longest x3 6.88 us: on_device(): upper.append(lax.ppermute(upper[-1] if upper else activated, 'embed', back))]
    reduce_scatter x1, waiting for transfers between devices: 51.3 us -> 56.4 us  [on_device(): lax.psum_scatter(partial_out, 'hy', scatter_dimension=0, tiled=True)]
    dot_general x1, matrix products: 2.33 us -> 5.14 us  [on_device(): gate_part = jnp.dot(piece, gate_weight, preferred_element_type=jnp.float32)]
    dot_general x1, matrix products: 5.14 us -> 2.33 us  [on_device(): up_part = jnp.dot(piece, up_weight, preferred_element_type=jnp.float32)]
  transfers between devices with their start and end apart: 4 -> 11, of which waited for: 4 -> 8; matrix products, arithmetic and copies ran while one was open for 0% -> 1% of each run, Pallas kernels for 0% -> 0%
where the time goes in v1:
time: 250 us
  waiting for transfers between devices  178 us (71%)
  blocking collectives  31.1 us (12%)
  matrix products  13.8 us (6%)
  between operations  13.2 us (5%)
  starting transfers between devices  7.03 us (3%)
  other arithmetic  5.88 us (2%)
    reduce_scatter x1, waiting for transfers between devices, on_device(): lax.psum_scatter(partial_out, 'hy', scatter_dimension=0, tiled=True)  56.4 us
    reduce_scatter x1, waiting for transfers between devices, on_device(): totals = lax.psum_scatter(totals, 'hz', scatter_dimension=0, tiled=True)  41 us
    reduce_scatter x1, waiting for transfers between devices, on_device(): lax.psum_scatter(partial_value, 'embed', scatter_dimension=0, tiled=True)  36.1 us
    all_gather x1, waiting for transfers between devices, on_device(): piece = lax.all_gather(piece, 'hy', axis=0, tiled=True)  33.1 us
    all_gather x1, blocking collectives, on_device(): piece = lax.all_gather(rows_in, 'hz', axis=0, tiled=True)  31.1 us
    ppermute x4, waiting for transfers between devices, on_device(): lax.ppermute(lower[-1] if lower else activated, 'embed', pairs)  11.3 us
    ppermute x3, starting transfers between devices, on_device(): upper.append(lax.ppermute(upper[-1] if upper else activated, 'embed', back))  6.88 us
    dot_general x1, matrix products, on_device(): jnp.dot(activated, down_weight, preferred_element_type=jnp.float32)  6.38 us
  transfers between devices with their start and end apart: 11, of which 8 were waited for; matrix products, arithmetic and copies ran while one was open for 1% of the time, Pallas kernels for 0%

profile of v1, /device:TPU:2, one launch (start us, length us, event | category | flops | bytes accessed | tf_op | source)
XLA Modules:
  0.0 249.9 jit_solution(2500144262496533329)
XLA Ops:
  6.5 31.1 %all_gather.6 = bf16[128,2048]{1,0:T(8,128)(2,1)} all-gather(bf16[16,2048]{1,0:T(8,128)(2,1)} %param.4), channel_id=1, replica_groups=mesh['embed'=8,'hy'=4,'hz'=8] {'hz'}, dimensions={0}, use_global_device_ids=true | all-gather | bytes 589824 | tf_op jit(solution)/shard_map/all_gather | solution.py:15
  37.6 0.0 all-gather.2.cloned.1.call-update
  37.7 0.0 reduce-scatter.4.cloned.1.call-start
  37.7 33.1 %all-gather.2.cloned.1.call-done = bf16[512,2048]{1,0:T(8,128)(2,1)} async-done(((bf16[128,2048]{1,0:T(8,128)(2,1)}), bf16[512,2048]{1,0:T(8,128)(2,1)}) %all-gather.2.cloned.1.call-update) | async-done | bytes 2097168 | tf_op jit(solution)/shard_map/all_gather | solution.py:16
  70.8 5.1 %fusion.3 = f32[512,896]{1,0:T(8,128)S(1)} fusion(bf16[512,2048]{1,0:T(8,128)(2,1)} %all-gather.2.cloned.1.call-done, bf16[2048,896]{1,0:T(8,128)(2,1)} %param.5), kind=kOutput, calls=%fused_computation.19 | convolution fusion | flops 1879048192 | bytes 7602176 | tf_op jit(solution)/shard_map/dot_general | solution.py:17
  76.0 2.3 fusion.4
  78.3 2.1 pad_maximum_fusion
  80.3 0.0 reduce-scatter.4.cloned.1.call-update
  80.4 0.0 reduce-scatter.6.cloned.1.call-start
  80.4 36.1 %reduce-scatter.4.cloned.1.call-done = f32[64,1792]{1,0:T(8,128)} async-done(((f32[512,1792]{1,0:T(8,128)}), f32[64,1792]{1,0:T(8,128)}) %reduce-scatter.4.cloned.1.call-update) | async-done | bytes 458768 | tf_op jit(solution)/shard_map/reduce_scatter | solution.py:20
  116.5 1.1 fusion
  117.6 0.0 collective-permute-start
  117.7 4.2 %collective-permute-done = bf16[64,896]{1,0:T(8,128)(2,1)S(1)} collective-permute-done((bf16[64,896]{1,0:T(8,128)(2,1)S(1)}, bf16[64,896]{1,0:T(8,128)(2,1)S(1)}, u32[]{:S(2)}, u32[]{:S(2)}) %collective-permute-start) | collective-permute-done | bytes 114720 | tf_op jit(solution)/shard_map/ppermute | solution.py:28
  121.9 0.0 collective-permute-start.1
  121.9 1.7 collective-permute-start.4
  123.6 2.5 collective-permute-done.1
  126.1 2.1 collective-permute-start.5
  128.2 2.3 collective-permute-done.2
  130.5 0.0 collective-permute-start.3
  130.5 0.0 collective-permute-done.5
  130.5 3.1 %collective-permute-start.6 = (bf16[64,896]{1,0:T(8,128)(2,1)S(1)}, bf16[64,896]{1,0:T(8,128)(2,1)S(1)}, u32[]{:S(2)}, u32[]{:S(2)}) collective-permute-start(bf16[64,896]{1,0:T(8,128)(2,1)S(1)} %collective-permute-done.5), channel_id=1, source_target_pairs={{32,0},{64,32},{96,64},{128,96},{160,128},{192,160},{224,192},{0,2... | collective-permute-start | bytes 344072 | tf_op jit(solution)/shard_map/ppermute | solution.py:30
  133.6 2.3 collective-permute-done.3
  136.0 1.1 bitcast_dynamic-update-slice_fusion.3
  137.2 0.0 collective-permute-done.6
  137.2 0.7 gather_fusion
  137.9 6.4 %fusion.5 = f32[512,2048]{1,0:T(8,128)} fusion(bf16[512,896]{1,0:T(8,128)(2,1)S(1)} %bitcast.25, bf16[896,2048]{1,0:T(8,128)(2,1)} %param.7), kind=kOutput, calls=%fused_computation.21 | convolution fusion | flops 1879048192 | bytes 8781824 | tf_op jit(solution)/shard_map/dot_general | solution.py:35
  144.3 0.0 reduce-scatter.6.cloned.1.call-update
  144.3 0.0 reduce-scatter.8.cloned.1.call-start
  144.4 56.4 %reduce-scatter.6.cloned.1.call-done = f32[128,2048]{1,0:T(8,128)} async-done(((f32[512,2048]{1,0:T(8,128)}), f32[128,2048]{1,0:T(8,128)}) %reduce-scatter.6.cloned.1.call-update) | async-done | bytes 1048592 | tf_op jit(solution)/shard_map/reduce_scatter | solution.py:36
  200.8 0.0 reduce-scatter.8.cloned.1.call-update
  200.8 41.0 %reduce-scatter.8.cloned.1.call-done = f32[16,2048]{1,0:T(8,128)} async-done(((f32[128,2048]{1,0:T(8,128)}), f32[16,2048]{1,0:T(8,128)}) %reduce-scatter.8.cloned.1.call-update) | async-done | bytes 131088 | tf_op jit(solution)/shard_map/reduce_scatter | solution.py:37
  241.8 1.5 convert_element_type.7
  (16 shorter events, 0.1 us)
Async XLA Ops:
  6.5 64.2 %all-gather.2.cloned.1.call-start = ((), (), s32[]{:S(2)}) async-start(), calls=%async_computation.3 | async-start | bytes 2621440 | tf_op jit(solution)/shard_map/all_gather | solution.py:16
  37.7 78.9 %reduce-scatter.4.cloned.1.call-start = ((), (), s32[]{:S(2)}) async-start(), calls=%async_computation.4 | async-start | bytes 4128768 | tf_op jit(solution)/shard_map/reduce_scatter | solution.py:20
  70.8 5.2 %copy-start = (bf16[2048,896]{1,0:T(8,128)(2,1)S(1)}, bf16[2048,896]{1,0:T(8,128)(2,1)}, u32[]{:S(2)}) copy-start(bf16[2048,896]{1,0:T(8,128)(2,1)} %param.6) | copy-start | bytes 11010052
  70.8 5.2 %copy-start.1 = (bf16[512,2048]{1,0:T(8,128)(2,1)S(1)}, bf16[512,2048]{1,0:T(8,128)(2,1)}, u32[]{:S(2)}) copy-start(bf16[512,2048]{1,0:T(8,128)(2,1)} %all-gather.2.cloned.1.call-done) | copy-start | bytes 6291460
  80.4 120.4 %reduce-scatter.6.cloned.1.call-start = ((), (), s32[]{:S(2)}) async-start(), calls=%async_computation.5 | async-start | bytes 5242880 | tf_op jit(solution)/shard_map/reduce_scatter | solution.py:36
  117.6 4.2 %collective-permute-start = (bf16[64,896]{1,0:T(8,128)(2,1)S(1)}, bf16[64,896]{1,0:T(8,128)(2,1)S(1)}, u32[]{:S(2)}, u32[]{:S(2)}) collective-permute-start(bf16[64,896]{1,0:T(8,128)(2,1)S(1)} %fusion), channel_id=1, source_target_pairs={{0,32},{32,64},{64,96},{96,128},{128,160},{160,192},{192,224},{224... | collective-permute-start | bytes 344072 | tf_op jit(solution)/shard_map/ppermute | solution.py:28
  121.9 4.2 %collective-permute-start.1 = (bf16[64,896]{1,0:T(8,128)(2,1)S(1)}, bf16[64,896]{1,0:T(8,128)(2,1)S(1)}, u32[]{:S(2)}, u32[]{:S(2)}) collective-permute-start(bf16[64,896]{1,0:T(8,128)(2,1)S(1)} %collective-permute-done), channel_id=1, source_target_pairs={{0,32},{32,64},{64,96},{96,128},{128,160},{160,192},{192,224},{224... | collective-permute-start | bytes 344072 | tf_op jit(solution)/shard_map/ppermute | solution.py:28
  121.9 4.2 %collective-permute-start.4 = (bf16[64,896]{1,0:T(8,128)(2,1)S(1)}, bf16[64,896]{1,0:T(8,128)(2,1)S(1)}, u32[]{:S(2)}, u32[]{:S(2)}) collective-permute-start(bf16[64,896]{1,0:T(8,128)(2,1)S(1)} %fusion), channel_id=1, source_target_pairs={{32,0},{64,32},{96,64},{128,96},{160,128},{192,160},{224,192},{0,2... | collective-permute-start | bytes 344072 | tf_op jit(solution)/shard_map/ppermute | solution.py:30
  126.1 4.4 %collective-permute-start.2 = (bf16[64,896]{1,0:T(8,128)(2,1)S(1)}, bf16[64,896]{1,0:T(8,128)(2,1)S(1)}, u32[]{:S(2)}, u32[]{:S(2)}) collective-permute-start(bf16[64,896]{1,0:T(8,128)(2,1)S(1)} %collective-permute-done.1), channel_id=1, source_target_pairs={{0,32},{32,64},{64,96},{96,128},{128,160},{160,192},{192,224},{224... | collective-permute-start | bytes 344072 | tf_op jit(solution)/shard_map/ppermute | solution.py:28
  126.1 4.4 %collective-permute-start.5 = (bf16[64,896]{1,0:T(8,128)(2,1)S(1)}, bf16[64,896]{1,0:T(8,128)(2,1)S(1)}, u32[]{:S(2)}, u32[]{:S(2)}) collective-permute-start(bf16[64,896]{1,0:T(8,128)(2,1)S(1)} %collective-permute-done.4), channel_id=1, source_target_pairs={{32,0},{64,32},{96,64},{128,96},{160,128},{192,160},{224,192},{0,2... | collective-permute-start | bytes 344072 | tf_op jit(solution)/shard_map/ppermute | solution.py:30
  130.5 5.4 %collective-permute-start.3 = (bf16[64,896]{1,0:T(8,128)(2,1)S(1)}, bf16[64,896]{1,0:T(8,128)(2,1)S(1)}, u32[]{:S(2)}, u32[]{:S(2)}) collective-permute-start(bf16[64,896]{1,0:T(8,128)(2,1)S(1)} %collective-permute-done.2), channel_id=1, source_target_pairs={{0,32},{32,64},{64,96},{96,128},{128,160},{160,192},{192,224},{224... | collective-permute-start | bytes 344072 | tf_op jit(solution)/shard_map/ppermute | solution.py:28
  130.5 6.6 %collective-permute-start.6 = (bf16[64,896]{1,0:T(8,128)(2,1)S(1)}, bf16[64,896]{1,0:T(8,128)(2,1)S(1)}, u32[]{:S(2)}, u32[]{:S(2)}) collective-permute-start(bf16[64,896]{1,0:T(8,128)(2,1)S(1)} %collective-permute-done.5), channel_id=1, source_target_pairs={{32,0},{64,32},{96,64},{128,96},{160,128},{192,160},{224,192},{0,2... | collective-permute-start | bytes 344072 | tf_op jit(solution)/shard_map/ppermute | solution.py:30
  144.3 97.5 %reduce-scatter.8.cloned.1.call-start = ((), (), s32[]{:S(2)}) async-start(), calls=%async_computation.6 | async-start | bytes 1179648 | tf_op jit(solution)/shard_map/reduce_scatter | solution.py:37
Sparse Core Ops, SparseCore 0:
  37.8 32.9 all-gather.1
  80.5 35.9 reduce-scatter.3
  144.4 56.3 reduce-scatter.5
  203.4 38.3 reduce-scatter.7
